TPU v7x, 256 devices: a whole 4x4x8 slice. The times are simulated.
256 devices in a mesh: dp: 32 (over y, z_hi, core), tensor: 8 (over z_lo, x).
Axes of the slice: x: 4, y: 4, z: 8 (z_hi: 4, z_lo: 2; z = z_hi * 2 + z_lo), core: 2. Of those that a mesh axis runs over, the one named last changes fastest.
Arguments:
- inputs: bfloat16 [32768, 2048], P(('dp', 'tensor')), may hold values from -6 to 6
- norm_gain: float32 [2048], replicated, may hold values from 0.1 to 1.9
- proj_weight: bfloat16 [2048, 3, 2048], P('dp', None, 'tensor'), may hold values from -0.125 to 0.125
- filters: float32 [3, 7, 2048], P(None, None, 'tensor'), may hold values from -2.4 to 2.4
- cotangent: bfloat16 [32768, 2048], P('dp', 'tensor'), may hold values from -18 to 18
Outputs:
- mixed: bfloat16 [32768, 2048], P('dp', 'tensor')
- grad_inputs: bfloat16 [32768, 2048], P(('dp', 'tensor'))
- grad_proj: bfloat16 [2048, 3, 2048], P('dp', None, 'tensor')
- grad_filters: float32 [3, 7, 2048], P(None, None, 'tensor')
- grad_gain: float32 [2048], replicated
All inputs are finite; a program needn't handle non-finite values.
Results may differ from a plain program's by a relative error of at most 0.02.
Values may be sent and summed in bfloat16 or wider, within the bound.
No kernel may reach another device: no remote copies, remote signals or barrier semaphores. Data moves between devices by JAX's collectives and lax.ppermute only.
A program may use at most 64 MiB of HBM per device.

v0:
```python
import jax
import jax.numpy as jnp
from jax import lax
from jax.sharding import PartitionSpec as P


def passed_along(shard, axis, by):
    size = lax.axis_size(axis)
    pairs = [(i, i + by) for i in range(size) if 0 <= i + by < size]
    return lax.ppermute(shard, axis, pairs)


def body(inputs, norm_gain, proj_weight, filters, cotangent):
    taps = filters.shape[1]
    width = taps - 1
    wide = inputs.astype(jnp.float32)
    inv_rms = lax.rsqrt(jnp.mean(wide * wide, axis=1, keepdims=True) + 1e-05)
    normed = (wide * inv_rms * norm_gain).astype(jnp.bfloat16)
    weights = lax.all_gather(proj_weight, "dp", axis=0, tiled=True)
    positions = lax.all_gather(normed, "tensor", axis=0, tiled=True)
    length = positions.shape[0]
    streams = jnp.einsum(
        "td,dsc->tsc", positions, weights, preferred_element_type=jnp.float32
    ).astype(jnp.bfloat16)
    before = passed_along(streams[length - width :], "dp", 1)
    extended = jnp.concatenate([before, streams], axis=0).astype(jnp.float32)
    conv = jnp.zeros(streams.shape, jnp.float32)
    for tap in range(taps):
        conv = conv + filters[:, tap, :] * extended[width - tap : width - tap + length]
    mixed = (conv[:, 0] * conv[:, 1] * conv[:, 2]).astype(jnp.bfloat16)
    grad_out = cotangent.astype(jnp.float32)
    grad_conv = jnp.stack(
        [
            grad_out * conv[:, 1] * conv[:, 2],
            grad_out * conv[:, 0] * conv[:, 2],
            grad_out * conv[:, 0] * conv[:, 1],
        ],
        axis=1,
    )
    after = passed_along(grad_conv[:width], "dp", -1)
    grad_extended = jnp.concatenate([grad_conv, after], axis=0)
    grad_acc = jnp.zeros(streams.shape, jnp.float32)
    for tap in range(taps):
        grad_acc = grad_acc + filters[:, tap, :] * grad_extended[tap : tap + length]
    grad_streams = grad_acc.astype(jnp.bfloat16)
    filter_local = jnp.stack(
        [
            jnp.sum(grad_conv * extended[width - tap : width - tap + length], axis=0)
            for tap in range(taps)
        ],
        axis=1,
    )
    normed_terms = jnp.einsum(
        "tsc,dsc->td", grad_streams, weights, preferred_element_type=jnp.float32
    )
    grad_normed = lax.psum_scatter(
        normed_terms.astype(jnp.bfloat16), "tensor", scatter_dimension=0, tiled=True
    ).astype(jnp.float32)
    weight_terms = jnp.einsum(
        "td,tsc->dsc", positions, grad_streams, preferred_element_type=jnp.float32
    )
    grad_proj = lax.psum_scatter(
        weight_terms.astype(jnp.bfloat16), "dp", scatter_dimension=0, tiled=True
    )
    scaled = norm_gain * grad_normed
    grad_inputs = inv_rms * (
        scaled - wide * inv_rms * inv_rms * jnp.mean(scaled * wide, axis=1, keepdims=True)
    )
    gain_local = jnp.sum(grad_normed * wide * inv_rms, axis=0)
    grad_filters = lax.psum(filter_local, "dp")
    grad_gain = lax.psum(gain_local, ("dp", "tensor"))
    return (mixed, grad_inputs.astype(jnp.bfloat16), grad_proj, grad_filters, grad_gain)


def solution(mesh):
    return jax.shard_map(
        body,
        mesh=mesh,
        in_specs=(
            P(("dp", "tensor"), None),
            P(),
            P("dp", None, "tensor"),
            P(None, None, "tensor"),
            P("dp", "tensor"),
        ),
        out_specs=(
            P("dp", "tensor"),
            P(("dp", "tensor"), None),
            P("dp", None, "tensor"),
            P(None, None, "tensor"),
            P(),
        ),
        check_vma=False,
    )
```

profile of v0, /device:TPU:1, one launch (start us, length us, event | category | flops | bytes accessed | tf_op | source)
XLA Modules:
  0.0 393.9 jit_solution(4973453960555978686)
XLA Ops:
  7.2 0.0 all-gather.5.cloned.1.call-start
  7.2 0.7 all-gather.5.cloned.1.call-update
  7.9 0.0 all-gather.3.cloned.1.call-start
  7.9 1.2 fusion.26
  9.2 2.0 fusion.20
  11.2 0.0 all-gather.3.cloned.1.call-update
  11.2 0.0 reduce-scatter.3.cloned.1.call-start
  11.3 1.0 fusion.30
  12.3 59.7 %all-gather.5.cloned.1.call-done = bf16[2048,3,256]{2,0,1:T(8,128)(2,1)} async-done(((bf16[64,3,256]{2,0,1:T(8,128)(2,1)}), bf16[2048,3,256]{2,0,1:T(8,128)(2,1)}) %all-gather.5.cloned.1.call-update) | async-done | bytes 3145744 | tf_op jit(solution)/shard_map/all_gather | solution.py:19
  72.0 54.9 %all-gather.3.cloned.1.call-done = bf16[1024,2048]{1,0:T(8,128)(2,1)} async-done(((bf16[128,2048]{1,0:T(8,128)(2,1)}), bf16[1024,2048]{1,0:T(8,128)(2,1)}) %all-gather.3.cloned.1.call-update) | async-done | bytes 4194320 | tf_op jit(solution)/shard_map/all_gather | solution.py:20
  126.9 6.6 %fusion.14 = bf16[1024,3,256]{2,0,1:T(8,128)(2,1)S(1)} fusion(bf16[2048,3,256]{2,0,1:T(8,128)(2,1)} %all-gather.5.cloned.1.call-done, bf16[1024,2048]{1,0:T(8,128)(2,1)} %all-gather.3.cloned.1.call-done), kind=kOutput, calls=%fused_computation.33 | convolution fusion | flops 3222011904 | bytes 8912896 | tf_op jit(solution)/shard_map/td,dsc->tsc/dot_general | solution.py:22
  133.5 4.7 %collective-permute-start = (bf16[6,3,256]{2,0,1:T(8,128)(2,1)S(1)}, bf16[6,3,256]{2,0,1:T(8,128)(2,1)S(1)}, u32[]{:S(2)}, u32[]{:S(2)}) collective-permute-start(bf16[6,3,256]{2,0,1:T(8,128)(2,1)S(1)} %slice.120), channel_id=1, source_target_pairs={{0,8},{8,16},{16,24},{24,32},{32,40},{40,48},{48,56},{56,64},{64,7... | collective-permute-start | bytes 27656 | tf_op jit(solution)/shard_map/ppermute | solution.py:10
  138.3 0.8 collective-permute-done
  139.1 0.3 maximum_convert_fusion
  139.4 0.0 copy-start.1
  139.4 2.6 multiply_add_fusion
  142.0 1.2 fusion.25
  143.2 2.9 multiply_reduce_fusion
  146.0 1.9 collective-permute-start.1
  148.0 4.8 %collective-permute-done.1 = f32[6,3,256]{2,0,1:T(8,128)S(1)} collective-permute-done((f32[6,3,256]{2,0,1:T(8,128)S(1)}, f32[6,3,256]{2,0,1:T(8,128)S(1)}, u32[]{:S(2)}, u32[]{:S(2)}) %collective-permute-start.1) | collective-permute-done | bytes 18464 | tf_op jit(solution)/shard_map/ppermute | solution.py:10
  152.8 0.2 pad_maximum_fusion
  153.0 2.7 fusion.8
  155.8 5.1 %bitcast_convert_fusion = bf16[1024,2048]{1,0:T(8,128)(2,1)} fusion(bf16[1024,3,256]{2,0,1:T(8,128)(2,1)S(1)} %fusion.8, bf16[2048,3,256]{2,0,1:T(8,128)(2,1)S(1)} %copy-done.3), kind=kOutput, calls=%fused_computation | convolution fusion | flops 3223322624 | bytes 8912896 | tf_op jit(solution)/shard_map/tsc,dsc->td/dot_general | solution.py:53
  160.8 0.0 reduce-scatter.3.cloned.1.call-update
  160.9 0.2 reduce-scatter.5.cloned.1.call-start
  161.1 7.5 %fusion.4 = bf16[2048,3,256]{2,0,1:T(8,128)(2,1)} fusion(bf16[1024,3,256]{2,0,1:T(8,128)(2,1)S(1)} %fusion.8, bf16[1024,2048]{1,0:T(8,128)(2,1)} %all-gather.3.cloned.1.call-done), kind=kOutput, calls=%fused_computation.5 | convolution fusion | flops 3222798336 | bytes 8912896 | tf_op jit(solution)/shard_map/td,tsc->dsc/dot_general | solution.py:59
  168.6 0.0 reduce-scatter.5.cloned.1.call-update
  168.7 135.1 %psum.14 = f32[3,7,256]{2,0,1:T(4,128)S(1)} all-reduce(f32[3,7,256]{2,0,1:T(4,128)S(1)} %constant_dynamic-update-slice_fusion), channel_id=1, replica_groups=mesh['dp'=32,'tensor'=8] {'dp'}, use_global_device_ids=true, to_apply=%region_11.0 | all-reduce | flops 5376 | bytes 43008 | tf_op jit(solution)/shard_map/psum | solution.py:70
  303.8 0.6 copy.12
  304.5 1.4 fusion.29
  305.8 79.3 %psum.15 = f32[2048]{0:T(1024)} all-reduce(f32[2048]{0:T(1024)S(1)} %get-tuple-element.17), channel_id=1, replica_groups=mesh['dp'=32,'tensor'=8] {'dp','tensor'}, use_global_device_ids=true, to_apply=%region_13.0 | all-reduce | flops 2048 | bytes 16384 | tf_op jit(solution)/shard_map/psum | solution.py:71
  385.2 2.2 fusion.23
  (24 shorter events, 0.1 us)
Async XLA Ops:
  7.2 64.9 %all-gather.5.cloned.1.call-start = ((), (), s32[]{:S(2)}) async-start(), calls=%async_computation.3 | async-start | bytes 3244032 | tf_op jit(solution)/shard_map/all_gather | solution.py:19
  7.9 119.0 %all-gather.3.cloned.1.call-start = ((), (), s32[]{:S(2)}) async-start(), calls=%async_computation.2 | async-start | bytes 4718592 | tf_op jit(solution)/shard_map/all_gather | solution.py:20
  11.2 293.2 %reduce-scatter.3.cloned.1.call-start = ((), (), s32[]{:S(2)}) async-start(), calls=%async_computation.4 | async-start | bytes 4718592 | tf_op jit(solution)/shard_map/reduce_scatter | solution.py:56
  133.5 5.5 %collective-permute-start = (bf16[6,3,256]{2,0,1:T(8,128)(2,1)S(1)}, bf16[6,3,256]{2,0,1:T(8,128)(2,1)S(1)}, u32[]{:S(2)}, u32[]{:S(2)}) collective-permute-start(bf16[6,3,256]{2,0,1:T(8,128)(2,1)S(1)} %slice.120), channel_id=1, source_target_pairs={{0,8},{8,16},{16,24},{24,32},{32,40},{40,48},{48,56},{56,64},{64,7... | collective-permute-start | bytes 27656 | tf_op jit(solution)/shard_map/ppermute | solution.py:10
  139.4 2.6 copy-start.1
  146.0 6.8 %collective-permute-start.1 = (f32[6,3,256]{2,0,1:T(8,128)S(1)}, f32[6,3,256]{2,0,1:T(8,128)S(1)}, u32[]{:S(2)}, u32[]{:S(2)}) collective-permute-start(f32[6,3,256]{2,0,1:T(8,128)S(1)} %slice.131), channel_id=1, source_target_pairs={{8,0},{16,8},{24,16},{32,24},{40,32},{48,40},{56,48},{64,56},{72,6... | collective-permute-start | bytes 55304 | tf_op jit(solution)/shard_map/ppermute | solution.py:10
  153.0 2.7 copy-start.3
  160.9 226.5 %reduce-scatter.5.cloned.1.call-start = ((), (), s32[]{:S(2)}) async-start(), calls=%async_computation.5 | async-start | bytes 3244032 | tf_op jit(solution)/shard_map/reduce_scatter | solution.py:62
  168.6 135.8 %copy-start = (bf16[128,2048]{1,0:T(8,128)(2,1)S(1)}, bf16[128,2048]{1,0:T(8,128)(2,1)}, u32[]{:S(2)}) copy-start(bf16[128,2048]{1,0:T(8,128)(2,1)} %param.5) | copy-start | bytes 1572868
  168.6 135.8 %copy-start.2 = (f32[2048]{0:T(1024)S(1)}, f32[2048]{0:T(1024)}, u32[]{:S(2)}) copy-start(f32[2048]{0:T(1024)} %param.6) | copy-start | bytes 24580
Sparse Core Ops, SparseCore 0:
  10.7 61.3 all-gather.4
  74.4 52.5 all-gather.2
  161.0 54.1 reduce-scatter.2
  219.5 92.7 reduce-scatter.4
where the time goes:
time: 394 us
  blocking collectives  214 us (54%)
  waiting for transfers between devices  121 us (31%)
  matrix products  19.2 us (5%)
  other arithmetic  16.6 us (4%)
  between operations  13.9 us (4%)
  starting transfers between devices  6.99 us (2%)
    psum x1, blocking collectives, body(): grad_filters = lax.psum(filter_local, 'dp')  135 us
    psum x1, blocking collectives, body(): grad_gain = lax.psum(gain_local, ('dp', 'tensor'))  79.3 us
    all_gather x1, waiting for transfers between devices, body(): weights = lax.all_gather(proj_weight, 'dp', axis=0, tiled=True)  59.7 us
    all_gather x1, waiting for transfers between devices, body(): positions = lax.all_gather(normed, 'tensor', axis=0, tiled=True)  54.9 us
  transfers between devices with their start and end apart: 6, of which 4 were waited for; matrix products, arithmetic and copies ran while one was open for 4% of the time, Pallas kernels for 0%

commit v1 on v0

--- a/solution.py
+++ b/solution.py
@@ -68,7 +68,7 @@
     )
     gain_local = jnp.sum(grad_normed * wide * inv_rms, axis=0)
     grad_filters = lax.psum(filter_local, "dp")
-    grad_gain = lax.psum(gain_local, ("dp", "tensor"))
+    grad_gain = lax.all_gather(gain_local, ("dp", "tensor")).sum(axis=0)
     return (mixed, grad_inputs.astype(jnp.bfloat16), grad_proj, grad_filters, grad_gain)
 
 

time: 394 us -> 1020 us (2.59)
  waiting for transfers between devices: 121 us -> 816 us
  blocking collectives: 214 us -> 137 us
    all_gather x0 -> x1, waiting for transfers between devices: none -> 548 us  [body(): grad_gain = lax.all_gather(gain_local, ('dp', 'tensor')).sum(axis=0)]
    reduce_scatter x1, waiting for transfers between devices: 0.01 us -> 94.1 us  [body(): lax.psum_scatter(weight_terms.astype(jnp.bfloat16), 'dp', scatter_dimensi...]
    psum x1 -> x0, blocking collectives: 79.3 us -> none  [body(): grad_gain = lax.psum(gain_local, ('dp', 'tensor'))]
    reduce_scatter x1, waiting for transfers between devices: 0.01 us -> 53.4 us  [body(): lax.psum_scatter(normed_terms.astype(jnp.bfloat16), 'tensor', scatter_dim...]
  transfers between devices with their start and end apart: 6 -> 7, of which waited for: 4 -> 7; matrix products, arithmetic and copies ran while one was open for 4% -> 2% of each run, Pallas kernels for 0% -> 0%
where the time goes in v1:
time: 1020 us; the launch traced here: 1010 us
  waiting for transfers between devices  816 us (80%)
  blocking collectives  137 us (13%)
  matrix products  19.1 us (2%)
  other arithmetic  16.9 us (2%)
  between operations  14 us (1%)
    all_gather x1, waiting for transfers between devices, body(): grad_gain = lax.all_gather(gain_local, ('dp', 'tensor')).sum(axis=0)  548 us
    psum x1, blocking collectives, body(): grad_filters = lax.psum(filter_local, 'dp')  137 us
    reduce_scatter x1, waiting for transfers between devices, body(): lax.psum_scatter(weight_terms.astype(jnp.bfloat16), 'dp', scatter_dimensi...  94.1 us
    all_gather x1, waiting for transfers between devices, body(): weights = lax.all_gather(proj_weight, 'dp', axis=0, tiled=True)  59.7 us
    all_gather x1, waiting for transfers between devices, body(): positions = lax.all_gather(normed, 'tensor', axis=0, tiled=True)  54.9 us
    reduce_scatter x1, waiting for transfers between devices, body(): lax.psum_scatter(normed_terms.astype(jnp.bfloat16), 'tensor', scatter_dim...  53.4 us
  transfers between devices with their start and end apart: 7, of which 7 were waited for; matrix products, arithmetic and copies ran while one was open for 2% of the time, Pallas kernels for 0%

profile of v1, /device:TPU:1, one launch (start us, length us, event | category | flops | bytes accessed | tf_op | source)
XLA Modules:
  0.0 1014.1 jit_solution(13233797212724266496)
XLA Ops:
  7.2 0.7 all-gather.7.cloned.1.call-update
  7.9 0.0 all-gather.5.cloned.1.call-start
  7.9 1.2 fusion.26
  9.2 2.0 fusion.20
  11.2 0.0 reduce-scatter.3.cloned.1.call-start
  11.3 1.0 fusion.30
  12.3 59.7 %all-gather.7.cloned.1.call-done = bf16[2048,3,256]{2,0,1:T(8,128)(2,1)} async-done(((bf16[64,3,256]{2,0,1:T(8,128)(2,1)}), bf16[2048,3,256]{2,0,1:T(8,128)(2,1)}) %all-gather.7.cloned.1.call-update) | async-done | bytes 3145744 | tf_op jit(solution)/shard_map/all_gather | solution.py:19
  72.0 54.9 %all-gather.5.cloned.1.call-done = bf16[1024,2048]{1,0:T(8,128)(2,1)} async-done(((bf16[128,2048]{1,0:T(8,128)(2,1)}), bf16[1024,2048]{1,0:T(8,128)(2,1)}) %all-gather.5.cloned.1.call-update) | async-done | bytes 4194320 | tf_op jit(solution)/shard_map/all_gather | solution.py:20
  126.9 6.6 fusion.14
  133.5 4.7 collective-permute-start
  138.3 0.8 collective-permute-done
  139.1 0.3 maximum_convert_fusion
  139.4 2.6 multiply_add_fusion
  142.0 1.2 fusion.25
  143.2 2.9 multiply_reduce_fusion
  146.1 1.9 collective-permute-start.1
  148.0 4.8 collective-permute-done.1
  152.8 0.2 pad_maximum_fusion
  153.1 2.7 fusion.8
  155.8 5.1 bitcast_convert_fusion
  160.9 0.0 all-gather.9.cloned.1.call-start
  160.9 53.4 %reduce-scatter.3.cloned.1.call-done = bf16[128,2048]{1,0:T(8,128)(2,1)} async-done(((bf16[1024,2048]{1,0:T(8,128)(2,1)}), bf16[128,2048]{1,0:T(8,128)(2,1)}) %reduce-scatter.3.cloned.1.call-update) | async-done | bytes 524304 | tf_op jit(solution)/shard_map/reduce_scatter | solution.py:56
  214.3 2.0 fusion.29
  216.3 0.2 reduce-scatter.5.cloned.1.call-start
  216.5 7.4 fusion.4
  224.0 137.2 %psum.7 = f32[3,7,256]{2,0,1:T(4,128)S(1)} all-reduce(f32[3,7,256]{2,0,1:T(4,128)S(1)} %constant_dynamic-update-slice_fusion), channel_id=1, replica_groups=mesh['dp'=32,'tensor'=8] {'dp'}, use_global_device_ids=true, to_apply=%region_11.0 | all-reduce | flops 5376 | bytes 43008 | tf_op jit(solution)/shard_map/psum | solution.py:70
  361.3 0.6 copy.16
  361.9 1.1 fusion.23
  363.0 548.0 %all-gather.9.cloned.1.call-done = f32[524288]{0:T(1024)} async-done(((f32[2048]{0:T(1024)}), f32[524288]{0:T(1024)}) %all-gather.9.cloned.1.call-update) | async-done | bytes 2097168 | tf_op jit(solution)/shard_map/all_gather | solution.py:71
  911.0 1.7 reshape.30
  912.8 0.7 reduce_sum.109
  913.5 94.1 %reduce-scatter.5.cloned.1.call-done = bf16[64,3,256]{2,0,1:T(8,128)(2,1)} async-done(((bf16[2048,3,256]{2,0,1:T(8,128)(2,1)}), bf16[64,3,256]{2,0,1:T(8,128)(2,1)}) %reduce-scatter.5.cloned.1.call-update) | async-done | bytes 98320 | tf_op jit(solution)/shard_map/reduce_scatter | solution.py:62
  (30 shorter events, 0.2 us)
Async XLA Ops:
  7.2 64.9 %all-gather.7.cloned.1.call-start = ((), (), s32[]{:S(2)}) async-start(), calls=%async_computation.3 | async-start | bytes 3244032 | tf_op jit(solution)/shard_map/all_gather | solution.py:19
  7.9 119.0 %all-gather.5.cloned.1.call-start = ((), (), s32[]{:S(2)}) async-start(), calls=%async_computation.2 | async-start | bytes 4718592 | tf_op jit(solution)/shard_map/all_gather | solution.py:20
  11.2 203.0 %reduce-scatter.3.cloned.1.call-start = ((), (), s32[]{:S(2)}) async-start(), calls=%async_computation.4 | async-start | bytes 4718592 | tf_op jit(solution)/shard_map/reduce_scatter | solution.py:56
  133.5 5.5 collective-permute-start
  139.4 2.6 copy-start.2
  146.1 6.8 collective-permute-start.1
  153.0 2.7 copy-start.4
  160.8 53.4 %copy-start = (bf16[128,2048]{1,0:T(8,128)(2,1)S(1)}, bf16[128,2048]{1,0:T(8,128)(2,1)}, u32[]{:S(2)}) copy-start(bf16[128,2048]{1,0:T(8,128)(2,1)} %param.5) | copy-start | bytes 1572868
  160.8 53.4 %copy-start.3 = (f32[2048]{0:T(1024)S(1)}, f32[2048]{0:T(1024)}, u32[]{:S(2)}) copy-start(f32[2048]{0:T(1024)} %param.6) | copy-start | bytes 24580
  160.9 750.2 %all-gather.9.cloned.1.call-start = ((), (), s32[]{:S(2)}) async-start(), calls=%async_computation.6 | async-start | bytes 2105344 | tf_op jit(solution)/shard_map/all_gather | solution.py:71
  216.3 791.3 %reduce-scatter.5.cloned.1.call-start = ((), (), s32[]{:S(2)}) async-start(), calls=%async_computation.5 | async-start | bytes 3244032 | tf_op jit(solution)/shard_map/reduce_scatter | solution.py:62
  223.9 138.0 %copy-start.1 = (bf16[128,2048]{1,0:T(8,128)(2,1)S(1)}, bf16[128,2048]{1,0:T(8,128)(2,1)}, u32[]{:S(2)}) copy-start(bf16[128,2048]{1,0:T(8,128)(2,1)} %reduce-scatter.3.cloned.1.call-done) | copy-start | bytes 1572868
Sparse Core Ops, SparseCore 0:
  10.7 61.3 all-gather.6
  74.4 52.5 all-gather.4
  161.0 53.2 reduce-scatter.2
  216.6 694.4 all-gather.8
  915.4 92.1 reduce-scatter.4
